TPU v7x, 512 devices: a whole 4x8x8 slice. The times are simulated.
512 devices in a mesh: dp: 8 (over x, core), expert: 64 (over z, y).
Axes of the slice: x: 4, y: 8, z: 8, core: 2. Of those that a mesh axis runs over, the one named last changes fastest.
Arguments:
- tokens: bfloat16 [65536, 512], P(('dp', 'expert')), may hold values from -6 to 6
- modality: int32 [65536], P(('dp', 'expert')), may hold values 0 or 1
- modal_gains: float32 [2, 512], replicated, may hold values from 0.5 to 2
- routes: int32 [65536, 2], P(('dp', 'expert')), may hold values from 0 to 63, all different within a row; in each aligned block of 128 rows (0 to 127, 128 to 255, ...) at most 8 rows name the same one
- gate_share: int32 [65536], P(('dp', 'expert')), may hold values from 1 to 15
- up_weight: bfloat16 [64, 2048, 512], P('expert', 'dp'), may hold values from -0.25 to 0.25
- down_weight: bfloat16 [64, 2048, 512], P('expert', 'dp'), may hold values from -0.125 to 0.125
- cotangent: bfloat16 [65536, 512], P(('dp', 'expert')), may hold values from -6 to 6
Outputs:
- moe_output: bfloat16 [65536, 512], P(('dp', 'expert'))
- token_grad: bfloat16 [65536, 512], P(('dp', 'expert'))
- up_grad: bfloat16 [64, 2048, 512], P('expert', 'dp')
- down_grad: bfloat16 [64, 2048, 512], P('expert', 'dp')
Inputs may be any that keep to these rules, and one draw needn't show every extreme that they name: `routes`: each row names two different experts; among the 128 rows of one device no expert is named more than 8 times, and in every draw some device names some expert exactly 8 times.
All inputs are finite; a program needn't handle non-finite values. No bound on the sum of `modality` on one device may be relied on, other than what follows from the above.
Results may differ from a plain program's by a relative error of at most 0.014.
Values may be sent and summed in bfloat16 or wider, within the bound.
No kernel may reach another device: no remote copies, remote signals or barrier semaphores. Data moves between devices by JAX's collectives and lax.ppermute only.
A program may use at most 64 MiB of HBM per device.

v0:
```python
import math
import jax
import jax.numpy as jnp
from jax import lax
from jax.sharding import PartitionSpec as P

root_half = 0.7071067811865476
density = 0.3989422804014327


def gelu_value(values):
    return values * 0.5 * (1.0 + lax.erf(values * root_half))


def gelu_slope(values):
    return (
        0.5 * (1.0 + lax.erf(values * root_half))
        + values * jnp.exp(-0.5 * values * values) * density
    )


def row_product(left_side, right_side, right_axis):
    numbers = (((1,), (right_axis,)), ((), ()))
    return lax.dot_general(left_side, right_side, numbers, preferred_element_type=jnp.float32)


def row_contract(left_side, right_side):
    numbers = (((0,), (0,)), ((), ()))
    return lax.dot_general(left_side, right_side, numbers, preferred_element_type=jnp.float32)


def on_device(tokens, modality, modal_gains, routes, gate_share, up_weight, down_weight, cotangent):
    tok_count = tokens.shape[0]
    model_width = tokens.shape[1]
    expert_count = lax.axis_size("expert")
    replica_count = lax.axis_size("x") * lax.axis_size("core")
    capacity = 4 * tok_count // expert_count
    slot_count = expert_count * capacity
    route_count = 2 * tok_count
    grad_scale = 1.0 / math.sqrt(2 * tok_count * replica_count)
    shard = jnp.concatenate([up_weight, down_weight], axis=0)
    whole = lax.all_gather(
        lax.all_gather(shard, "x", axis=1, tiled=True), "core", axis=1, tiled=True
    )
    whole_up, whole_down = (whole[0], whole[1])
    x_float = tokens.astype(jnp.float32)
    inv_rms = lax.rsqrt(jnp.mean(x_float * x_float, axis=-1, keepdims=True) + 1e-06)
    gain_rows = jnp.where(modality[:, None] == 1, modal_gains[1][None, :], modal_gains[0][None, :])
    normed = (x_float * inv_rms * gain_rows).astype(jnp.bfloat16)
    gate_first = gate_share.astype(jnp.float32) / 16.0
    flat_routes = routes.reshape(-1)
    one_hot = flat_routes[:, None] == jnp.arange(expert_count, dtype=jnp.int32)[None, :]
    route_ids = jnp.arange(route_count, dtype=jnp.int32)
    before = (route_ids[None, :] < route_ids[:, None]).astype(jnp.bfloat16)
    earlier = jnp.dot(before, one_hot.astype(jnp.bfloat16), preferred_element_type=jnp.float32)
    position = jnp.sum(jnp.where(one_hot, earlier, 0.0), axis=1).astype(jnp.int32)
    slot_index = (flat_routes * capacity + position).reshape(tok_count, 2)
    slot_ids = jnp.arange(slot_count, dtype=jnp.int32)[:, None]
    first_hit = slot_ids == slot_index[:, 0][None, :]
    second_hit = slot_ids == slot_index[:, 1][None, :]
    pick = (first_hit | second_hit).astype(jnp.bfloat16)
    weigh = jnp.where(
        first_hit, gate_first[None, :], jnp.where(second_hit, 1.0 - gate_first[None, :], 0.0)
    ).astype(jnp.bfloat16)
    pick = pick.reshape(expert_count, 1, capacity, tok_count)
    weigh = weigh.reshape(expert_count, 1, capacity, tok_count)
    blank = jnp.zeros_like(pick)
    gather_side = jnp.concatenate(
        [jnp.concatenate([pick, blank], axis=3), jnp.concatenate([blank, weigh], axis=3)], axis=1
    ).reshape(2 * slot_count, 2 * tok_count)
    return_side = jnp.concatenate(
        [jnp.concatenate([weigh, blank], axis=3), jnp.concatenate([blank, pick], axis=3)], axis=1
    ).reshape(2 * slot_count, 2 * tok_count)
    sources = jnp.concatenate([normed, cotangent], axis=0)
    sending = jnp.dot(gather_side, sources, preferred_element_type=jnp.float32).astype(jnp.bfloat16)
    arrived = lax.all_to_all(
        sending.reshape(expert_count, 2 * capacity, model_width),
        "expert",
        split_axis=0,
        concat_axis=0,
        tiled=True,
    )
    expert_rows = arrived[:, :capacity].reshape(slot_count, model_width)
    grad_rows = arrived[:, capacity:].reshape(slot_count, model_width)
    pre_act = row_product(expert_rows, whole_up, 1)
    activated = gelu_value(pre_act).astype(jnp.bfloat16)
    expert_out = row_product(activated, whole_down, 0).astype(jnp.bfloat16)
    hidden_grad = row_product(grad_rows, whole_down, 1)
    pre_grad = (hidden_grad * gelu_slope(pre_act)).astype(jnp.bfloat16)
    normed_part = row_product(pre_grad, whole_up, 0).astype(jnp.bfloat16)
    leaving = jnp.concatenate(
        [
            expert_out.reshape(expert_count, capacity, model_width),
            normed_part.reshape(expert_count, capacity, model_width),
        ],
        axis=1,
    )
    back = lax.all_to_all(leaving, "expert", split_axis=0, concat_axis=0, tiled=True)
    up_term = row_contract(pre_grad, expert_rows) * grad_scale
    down_term = row_contract(activated, grad_rows) * grad_scale
    parts = jnp.stack([up_term, down_term], axis=1).astype(jnp.bfloat16)
    grad_pair = lax.psum_scatter(
        lax.psum_scatter(parts, "core", scatter_dimension=0, tiled=True),
        "x",
        scatter_dimension=0,
        tiled=True,
    )
    up_grad = grad_pair[:, 0][None]
    down_grad = grad_pair[:, 1][None]
    combined = row_contract(return_side, back.reshape(2 * slot_count, model_width))
    moe_output = combined[:tok_count].astype(jnp.bfloat16)
    normed_grad = combined[tok_count:]
    scaled = gain_rows * normed_grad
    token_grad = (
        inv_rms * scaled - x_float * inv_rms**3 * jnp.mean(x_float * scaled, axis=-1, keepdims=True)
    ).astype(jnp.bfloat16)
    return (moe_output, token_grad, up_grad, down_grad)


def solution(mesh):
    dp_size, expert_size = mesh.devices.shape
    cores = 2
    mesh = jax.sharding.Mesh(
        mesh.devices.reshape(dp_size // cores, cores, expert_size), ("x", "core", "expert")
    )
    placed = (
        P(("x", "core", "expert"), None),
        P(("x", "core", "expert")),
        P(),
        P(("x", "core", "expert"), None),
        P(("x", "core", "expert")),
        P("expert", ("x", "core"), None),
        P("expert", ("x", "core"), None),
        P(("x", "core", "expert"), None),
    )
    return jax.shard_map(
        on_device,
        mesh=mesh,
        in_specs=placed,
        out_specs=(
            P(("x", "core", "expert"), None),
            P(("x", "core", "expert"), None),
            P("expert", ("x", "core"), None),
            P("expert", ("x", "core"), None),
        ),
        check_vma=False,
    )
```

profile of v0, /device:TPU:6, one launch (start us, length us, event | category | flops | bytes accessed | tf_op | source)
XLA Modules:
  0.0 178.2 jit_solution(408768301681310758)
XLA Ops:
  7.3 1.9 %pad_maximum_fusion.2 = bf16[2,256,512]{2,1,0:T(8,128)(2,1)} fusion(bf16[1,256,512]{2,1,0:T(8,128)(2,1)} %param.14, bf16[1,256,512]{2,1,0:T(8,128)(2,1)} %param.13), kind=kLoop, calls=%fused_computation.37 | loop fusion | flops 262144 | bytes 1048576 | tf_op jit(solution)/shard_map/concatenate | solution.py:41
  9.3 0.8 copy.18
  10.1 0.1 eq.88
  10.2 0.2 fusion.15
  10.6 0.7 convert_multiply_fusion.4
  11.3 0.7 multiply_add_fusion.1
  12.0 37.1 %all-gather.3.cloned.1.call-done = bf16[2,1024,512]{2,1,0:T(8,128)(2,1)} async-done(((bf16[2,256,512]{2,1,0:T(8,128)(2,1)}), bf16[2,1024,512]{2,1,0:T(8,128)(2,1)}) %all-gather.3.cloned.1.call-update) | async-done | bytes 2097168 | tf_op jit(solution)/shard_map/all_gather | solution.py:43
  49.9 0.4 convolution_convert_fusion
  50.3 42.9 %all_to_all.10 = bf16[64,16,512]{2,1,0:T(8,128)(2,1)S(1)} all-to-all(bf16[64,16,512]{2,1,0:T(8,128)(2,1)S(1)} %bitcast.57), channel_id=1, replica_groups=mesh['x'=4,'core'=2,'expert'=64] {'expert'}, dimensions={0} | all-to-all | bytes 2097152 | tf_op jit(solution)/shard_map/all_to_all | solution.py:76
  93.2 3.1 %multiply_convert_fusion.2 = (bf16[512,2048]{1,0:T(8,128)(2,1)S(1)}, f32[512,2048]{1,0:T(8,128)S(1)}) fusion(bf16[2,2048,512]{2,1,0:T(8,128)(2,1)} %all-gather.5.cloned.1.call-done, bf16[64,16,512]{2,1,0:T(8,128)(2,1)S(1)} %all_to_all.10), kind=kOutput, calls=%fused_computation.10 | convolution fusion | flops 1078984704 | bytes 8912896 | tf_op jit(solution)/shard_map/dot_general | solution.py:24
  96.3 2.8 %fusion.5 = bf16[512,2048]{1,0:T(8,128)(2,1)S(1)} fusion(f32[512,2048]{1,0:T(8,128)S(1)} %get-tuple-element.17, bf16[2,2048,512]{2,1,0:T(8,128)(2,1)S(1)} %copy-done.3, bf16[64,16,512]{2,1,0:T(8,128)(2,1)S(1)} %all_to_all.10), kind=kOutput, calls=%fused_computation.6 | convolution fusion | flops 1084227584 | bytes 8912896 | tf_op jit(solution)/shard_map/dot_general | solution.py:24
  99.2 1.3 fusion.7
  100.5 1.3 fusion.6
  101.8 2.3 %pad_maximum_fusion = bf16[2048,2,512]{2,0,1:T(8,128)(2,1)} fusion(bf16[2048,1,512]{2,0,1:T(8,128)(2,1)S(1)} %fusion.7, bf16[2048,1,512]{2,0,1:T(8,128)(2,1)S(1)} %fusion.6), kind=kLoop, calls=%fused_computation.7 | loop fusion | flops 2097152 | bytes 8388608 | tf_op jit(solution)/shard_map/stack | solution.py:101
  104.2 15.5 %reduce-scatter.3.cloned.1.call-done = bf16[1024,2,512]{2,0,1:T(8,128)(2,1)} async-done(((bf16[2048,2,512]{2,0,1:T(8,128)(2,1)}), bf16[1024,2,512]{2,0,1:T(8,128)(2,1)}) %reduce-scatter.3.cloned.1.call-update) | async-done | bytes 2097168 | tf_op jit(solution)/shard_map/reduce_scatter | solution.py:103
  119.8 3.0 %fusion.13 = bf16[64,8,512]{2,1,0:T(8,128)(2,1)S(1)} fusion(bf16[512,2048]{1,0:T(8,128)(2,1)S(1)} %copy-done.9, bf16[2,2048,512]{2,1,0:T(8,128)(2,1)} %all-gather.5.cloned.1.call-done), kind=kOutput, calls=%fused_computation.22 | convolution fusion | flops 1074003968 | bytes 4718592 | tf_op jit(solution)/shard_map/dot_general | solution.py:24
  122.8 0.5 copy-done.7
  123.2 1.2 fusion.14
  124.6 43.0 %all_to_all.11 = bf16[64,16,512]{2,1,0:T(8,128)(2,1)S(1)} all-to-all(bf16[64,16,512]{2,1,0:T(8,128)(2,1)S(1)} %pad_maximum_fusion.1), channel_id=1, replica_groups=mesh['x'=4,'core'=2,'expert'=64] {'expert'}, dimensions={0} | all-to-all | bytes 2097152 | tf_op jit(solution)/shard_map/all_to_all | solution.py:98
  167.6 0.4 fusion.36
  168.1 0.7 slice.87
  168.8 0.2 fusion.28
  169.0 0.8 fusion.27
  169.8 1.9 %slice_bitcast_fusion.20 = (bf16[1,256,512]{2,1,0:T(8,128)(2,1)}, bf16[1,256,512]{2,1,0:T(8,128)(2,1)}) fusion(bf16[256,2,512]{2,0,1:T(8,128)(2,1)} %reduce-scatter.5.cloned.1.call-done), kind=kLoop, calls=%fused_computation.54 | loop fusion | bytes 1048576 | tf_op jit(solution)/shard_map/broadcast_in_dim;squeeze | solution.py:109
  (44 shorter events, 1.2 us)
Async XLA Ops:
  7.2 42.0 %copy-start = (bf16[128,512]{1,0:T(8,128)(2,1)S(1)}, bf16[128,512]{1,0:T(8,128)(2,1)}, u32[]{:S(2)}) copy-start(bf16[128,512]{1,0:T(8,128)(2,1)} %param.8) | copy-start | bytes 393220
  7.2 42.5 %copy-start.5 = (s32[128]{0:T(128)S(1)}, s32[128]{0:T(128)}, u32[]{:S(2)}) copy-start(s32[128]{0:T(128)} %param.9) | copy-start | bytes 1540
  7.2 42.6 %copy-start.2 = (f32[2,512]{1,0:T(2,128)S(1)}, f32[2,512]{1,0:T(2,128)}, u32[]{:S(2)}) copy-start(f32[2,512]{1,0:T(2,128)} %param.10) | copy-start | bytes 12292
  7.2 42.7 %copy-start.1 = (bf16[128,512]{1,0:T(8,128)(2,1)S(1)}, bf16[128,512]{1,0:T(8,128)(2,1)}, u32[]{:S(2)}) copy-start(bf16[128,512]{1,0:T(8,128)(2,1)} %param.15) | copy-start | bytes 393220
  7.2 41.9 %all-gather.3.cloned.1.call-start = ((), (), s32[]{:S(2)}) async-start(), calls=%async_computation.4 | async-start | bytes 2621440 | tf_op jit(solution)/shard_map/all_gather | solution.py:43
  9.2 84.0 %all-gather.5.cloned.1.call-start = ((), (), s32[]{:S(2)}) async-start(), calls=%async_computation.5 | async-start | bytes 6291456 | tf_op jit(solution)/shard_map/all_gather | solution.py:42
  49.1 70.6 %reduce-scatter.3.cloned.1.call-start = ((), (), s32[]{:S(2)}) async-start(), calls=%async_computation.6 | async-start | bytes 6291456 | tf_op jit(solution)/shard_map/reduce_scatter | solution.py:103
  93.2 3.1 %copy-start.3 = (bf16[2,2048,512]{2,1,0:T(8,128)(2,1)S(1)}, bf16[2,2048,512]{2,1,0:T(8,128)(2,1)}, u32[]{:S(2)}) copy-start(bf16[2,2048,512]{2,1,0:T(8,128)(2,1)} %all-gather.5.cloned.1.call-done) | copy-start | bytes 12582916
  96.3 2.9 %copy-start.6 = (bf16[512,2048]{1,0:T(8,128)(2,1)}, bf16[512,2048]{1,0:T(8,128)(2,1)S(1)}, u32[]{:S(2)}) copy-start(bf16[512,2048]{1,0:T(8,128)(2,1)S(1)} %get-tuple-element.16) | copy-start | bytes 6291460
  99.1 1.3 copy-start.8
  104.1 15.6 %copy-start.9 = (bf16[512,2048]{1,0:T(8,128)(2,1)S(1)}, bf16[512,2048]{1,0:T(8,128)(2,1)}, u32[]{:S(2)}) copy-start(bf16[512,2048]{1,0:T(8,128)(2,1)} %copy-done.8) | copy-start | bytes 6291460
  104.2 65.6 %reduce-scatter.5.cloned.1.call-start = ((), (), s32[]{:S(2)}) async-start(), calls=%async_computation.7 | async-start | bytes 2621440 | tf_op jit(solution)/shard_map/reduce_scatter | solution.py:102
  119.7 3.0 %copy-start.4 = (bf16[2,2048,512]{2,1,0:T(8,128)(2,1)S(1)}, bf16[2,2048,512]{2,1,0:T(8,128)(2,1)}, u32[]{:S(2)}) copy-start(bf16[2,2048,512]{2,1,0:T(8,128)(2,1)} %all-gather.5.cloned.1.call-done) | copy-start | bytes 12582916
  119.7 3.5 %copy-start.7 = (bf16[512,2048]{1,0:T(8,128)(2,1)S(1)}, bf16[512,2048]{1,0:T(8,128)(2,1)}, u32[]{:S(2)}) copy-start(bf16[512,2048]{1,0:T(8,128)(2,1)} %copy-done.6) | copy-start | bytes 6291460
Sparse Core Ops, SparseCore 0:
  10.1 38.8 all-gather.2
  51.2 23.7 all-gather.4
  104.3 15.3 reduce-scatter.2
  122.6 34.4 reduce-scatter.4
where the time goes:
time: 178 us
  blocking collectives  85.9 us (48%)
  waiting for transfers between devices  52.6 us (30%)
  between operations  14.1 us (8%)
  matrix products  13.9 us (8%)
  other arithmetic  7.37 us (4%)
  local copies, waits for them, and re-layouts  4.15 us (2%)
    all_to_all x1, blocking collectives, on_device(): lax.all_to_all(leaving, 'expert', split_axis=0, concat_axis=0, tiled=True)  43 us
    all_to_all x1, blocking collectives, on_device(): lax.all_to_all(sending.reshape(expert_count, 2 * capacity, model_width),...  42.9 us
    all_gather x1, waiting for transfers between devices, on_device(): lax.all_gather(shard, 'x', axis=1, tiled=True)  37.1 us
    reduce_scatter x1, waiting for transfers between devices, on_device(): lax.psum_scatter(parts, 'core', scatter_dimension=0, tiled=True)  15.5 us
    dot_general x4, matrix products, row_product(): lax.dot_general(left_side, right_side, numbers, preferred_element_type=jn...  10.1 us
  transfers between devices with their start and end apart: 4, of which 2 were waited for; matrix products, arithmetic and copies ran while one was open for 6% of the time, Pallas kernels for 0%

commit v1 on v0

--- a/solution.py
+++ b/solution.py
@@ -40,7 +40,10 @@
     grad_scale = 1.0 / math.sqrt(2 * tok_count * replica_count)
     shard = jnp.concatenate([up_weight, down_weight], axis=0)
     whole = lax.all_gather(
-        lax.all_gather(shard, "x", axis=1, tiled=True), "core", axis=1, tiled=True
+        jnp.concatenate(lax.all_to_all(jnp.stack([shard] * lax.axis_size("x")), "x", 0, 0), axis=1),
+        "core",
+        axis=1,
+        tiled=True,
     )
     whole_up, whole_down = (whole[0], whole[1])
     x_float = tokens.astype(jnp.float32)

time: 178 us -> 171 us (0.961)
  waiting for transfers between devices: 52.6 us -> 33.4 us
  starting transfers between devices: 0.16 us -> 9.52 us
  local copies, waits for them, and re-layouts: 4.15 us -> 6.59 us
  other arithmetic: 7.37 us -> 5.17 us
  blocking collectives: 85.9 us -> 88.1 us
    all_gather x2 -> x1, waiting for transfers between devices: 37.1 us -> 0.01 us  [on_device(): lax.all_gather(jnp.concatenate(lax.all_to_all(jnp.stack([shard] * lax.axi...]
    all_to_all x0 -> x1, waiting for transfers between devices: none -> 18.8 us  [on_device(): lax.all_to_all(jnp.stack([shard] * lax.axis_size('x')), 'x', 0, 0)]
    all_to_all x0 -> x1, starting transfers between devices: none -> 9.43 us  [on_device(): lax.all_to_all(jnp.stack([shard] * lax.axis_size('x')), 'x', 0, 0)]
    all_to_all x1, blocking collectives: 42.9 us -> 45 us  [on_device(): lax.all_to_all(sending.reshape(expert_count, 2 * capacity, model_width),...]
  transfers between devices with their start and end apart: 4 -> 4, of which waited for: 2 -> 2; matrix products, arithmetic and copies ran while one was open for 6% -> 5% of each run, Pallas kernels for 0% -> 0%
where the time goes in v1:
time: 171 us
  blocking collectives  88.1 us (52%)
  waiting for transfers between devices  33.4 us (20%)
  between operations  14.1 us (8%)
  matrix products  13.9 us (8%)
  starting transfers between devices  9.52 us (6%)
  local copies, waits for them, and re-layouts  6.59 us (4%)
  other arithmetic  5.17 us (3%)
    all_to_all x1, blocking collectives, on_device(): lax.all_to_all(sending.reshape(expert_count, 2 * capacity, model_width),...  45 us
    all_to_all x1, blocking collectives, on_device(): lax.all_to_all(leaving, 'expert', split_axis=0, concat_axis=0, tiled=True)  43.1 us
    all_to_all x1, waiting for transfers between devices, on_device(): lax.all_to_all(jnp.stack([shard] * lax.axis_size('x')), 'x', 0, 0)  18.8 us
    reduce_scatter x1, waiting for transfers between devices, on_device(): lax.psum_scatter(parts, 'core', scatter_dimension=0, tiled=True)  14.5 us
    dot_general x4, matrix products, row_product(): lax.dot_general(left_side, right_side, numbers, preferred_element_type=jn...  10.1 us
    all_to_all x1, starting transfers between devices, on_device(): lax.all_to_all(jnp.stack([shard] * lax.axis_size('x')), 'x', 0, 0)  9.43 us
  transfers between devices with their start and end apart: 4, of which 2 were waited for; matrix products, arithmetic and copies ran while one was open for 5% of the time, Pallas kernels for 0%

profile of v1, /device:TPU:6, one launch (start us, length us, event | category | flops | bytes accessed | tf_op | source)
XLA Modules:
  0.0 170.7 jit_solution(7470323636594946946)
XLA Ops:
  7.2 1.1 pad_maximum_fusion.2
  8.3 1.5 stack.19
  9.8 9.4 %all-to-all-start.1 = ((bf16[4,2,256,512]{3,2,1,0:T(8,128)(2,1)}), bf16[4,2,256,512]{3,2,1,0:T(8,128)(2,1)S(1)}, u32[]{:S(2)}, u32[]{:S(2)}) async-start(bf16[4,2,256,512]{3,2,1,0:T(8,128)(2,1)} %stack.19), calls=%async_computation.1 | async-start | bytes 4194304 | tf_op jit(solution)/shard_map/all_to_all | solution.py:43
  19.3 0.1 eq.88
  19.5 0.2 fusion.15
  20.0 18.8 %all-to-all-done.1 = bf16[4,2,256,512]{3,2,1,0:T(8,128)(2,1)S(1)} async-done(((bf16[4,2,256,512]{3,2,1,0:T(8,128)(2,1)}), bf16[4,2,256,512]{3,2,1,0:T(8,128)(2,1)S(1)}, u32[]{:S(2)}, u32[]{:S(2)}) %all-to-all-start.1) | async-done | bytes 2097184 | tf_op jit(solution)/shard_map/all_to_all | solution.py:43
  38.8 1.6 copy.24
  41.2 0.4 convolution_convert_fusion
  41.6 45.0 %all_to_all.15 = bf16[64,16,512]{2,1,0:T(8,128)(2,1)S(1)} all-to-all(bf16[64,16,512]{2,1,0:T(8,128)(2,1)S(1)} %bitcast.61), channel_id=1, replica_groups=mesh['x'=4,'core'=2,'expert'=64] {'expert'}, dimensions={0} | all-to-all | bytes 2097152 | tf_op jit(solution)/shard_map/all_to_all | solution.py:79
  86.7 3.1 %multiply_convert_fusion.2 = (bf16[512,2048]{1,0:T(8,128)(2,1)S(1)}, f32[512,2048]{1,0:T(8,128)S(1)}) fusion(bf16[2,2048,512]{2,1,0:T(8,128)(2,1)} %all-gather.2.cloned.1.call-done, bf16[64,16,512]{2,1,0:T(8,128)(2,1)S(1)} %all_to_all.15), kind=kOutput, calls=%fused_computation.10 | convolution fusion | flops 1078984704 | bytes 8912896 | tf_op jit(solution)/shard_map/dot_general | solution.py:24
  89.8 2.8 %fusion.5 = bf16[512,2048]{1,0:T(8,128)(2,1)S(1)} fusion(f32[512,2048]{1,0:T(8,128)S(1)} %get-tuple-element.17, bf16[2,2048,512]{2,1,0:T(8,128)(2,1)S(1)} %copy-done.4, bf16[64,16,512]{2,1,0:T(8,128)(2,1)S(1)} %all_to_all.15), kind=kOutput, calls=%fused_computation.6 | convolution fusion | flops 1084227584 | bytes 8912896 | tf_op jit(solution)/shard_map/dot_general | solution.py:24
  92.6 1.3 fusion.7
  93.9 1.3 fusion.6
  95.3 2.3 %pad_maximum_fusion = bf16[2048,2,512]{2,0,1:T(8,128)(2,1)} fusion(bf16[2048,1,512]{2,0,1:T(8,128)(2,1)S(1)} %fusion.7, bf16[2048,1,512]{2,0,1:T(8,128)(2,1)S(1)} %fusion.6), kind=kLoop, calls=%fused_computation.7 | loop fusion | flops 2097152 | bytes 8388608 | tf_op jit(solution)/shard_map/stack | solution.py:104
  97.7 14.5 %reduce-scatter.3.cloned.1.call-done = bf16[1024,2,512]{2,0,1:T(8,128)(2,1)} async-done(((bf16[2048,2,512]{2,0,1:T(8,128)(2,1)}), bf16[1024,2,512]{2,0,1:T(8,128)(2,1)}) %reduce-scatter.3.cloned.1.call-update) | async-done | bytes 2097168 | tf_op jit(solution)/shard_map/reduce_scatter | solution.py:106
  112.2 3.0 %fusion.13 = bf16[64,8,512]{2,1,0:T(8,128)(2,1)S(1)} fusion(bf16[512,2048]{1,0:T(8,128)(2,1)S(1)} %copy-done.11, bf16[2,2048,512]{2,1,0:T(8,128)(2,1)} %all-gather.2.cloned.1.call-done), kind=kOutput, calls=%fused_computation.22 | convolution fusion | flops 1074003968 | bytes 4718592 | tf_op jit(solution)/shard_map/dot_general | solution.py:24
  115.2 0.5 copy-done.9
  115.7 1.2 fusion.14
  117.0 43.1 %all_to_all.16 = bf16[64,16,512]{2,1,0:T(8,128)(2,1)S(1)} all-to-all(bf16[64,16,512]{2,1,0:T(8,128)(2,1)S(1)} %pad_maximum_fusion.1), channel_id=1, replica_groups=mesh['x'=4,'core'=2,'expert'=64] {'expert'}, dimensions={0} | all-to-all | bytes 2097152 | tf_op jit(solution)/shard_map/all_to_all | solution.py:101
  160.1 0.4 fusion.36
  160.6 0.7 slice.87
  161.3 0.2 fusion.28
  161.5 0.8 fusion.27
  162.3 1.9 %slice_bitcast_fusion.20 = (bf16[1,256,512]{2,1,0:T(8,128)(2,1)}, bf16[1,256,512]{2,1,0:T(8,128)(2,1)}) fusion(bf16[256,2,512]{2,0,1:T(8,128)(2,1)} %reduce-scatter.5.cloned.1.call-done), kind=kLoop, calls=%fused_computation.54 | loop fusion | bytes 1048576 | tf_op jit(solution)/shard_map/broadcast_in_dim;squeeze | solution.py:112
  (49 shorter events, 1.3 us)
Async XLA Ops:
  7.2 12.1 %copy-start.2 = (s32[128,2]{0,1:T(2,128)S(1)}, s32[128,2]{0,1:T(2,128)}, u32[]{:S(2)}) copy-start(s32[128,2]{0,1:T(2,128)} %param.11) | copy-start | bytes 3076
  7.2 12.8 %copy-start.6 = (s32[128]{0:T(128)S(1)}, s32[128]{0:T(128)}, u32[]{:S(2)}) copy-start(s32[128]{0:T(128)} %param.12) | copy-start | bytes 1540
  9.8 29.0 %all-to-all-start.1 = ((bf16[4,2,256,512]{3,2,1,0:T(8,128)(2,1)}), bf16[4,2,256,512]{3,2,1,0:T(8,128)(2,1)S(1)}, u32[]{:S(2)}, u32[]{:S(2)}) async-start(bf16[4,2,256,512]{3,2,1,0:T(8,128)(2,1)} %stack.19), calls=%async_computation.1 | async-start | bytes 4194304 | tf_op jit(solution)/shard_map/all_to_all | solution.py:43
  19.2 21.3 %copy-start = (bf16[128,512]{1,0:T(8,128)(2,1)S(1)}, bf16[128,512]{1,0:T(8,128)(2,1)}, u32[]{:S(2)}) copy-start(bf16[128,512]{1,0:T(8,128)(2,1)} %param.8) | copy-start | bytes 393220
  19.2 67.4 %all-gather.2.cloned.1.call-start = ((), (), s32[]{:S(2)}) async-start(), calls=%async_computation.5 | async-start | bytes 6291456 | tf_op jit(solution)/shard_map/all_gather | solution.py:42
  19.5 21.5 %copy-start.7 = (s32[128]{0:T(128)S(1)}, s32[128]{0:T(128)}, u32[]{:S(2)}) copy-start(s32[128]{0:T(128)} %param.9) | copy-start | bytes 1540
  19.5 21.6 %copy-start.3 = (f32[2,512]{1,0:T(2,128)S(1)}, f32[2,512]{1,0:T(2,128)}, u32[]{:S(2)}) copy-start(f32[2,512]{1,0:T(2,128)} %param.10) | copy-start | bytes 12292
  20.0 21.2 %copy-start.1 = (bf16[128,512]{1,0:T(8,128)(2,1)S(1)}, bf16[128,512]{1,0:T(8,128)(2,1)}, u32[]{:S(2)}) copy-start(bf16[128,512]{1,0:T(8,128)(2,1)} %param.15) | copy-start | bytes 393220
  40.4 71.7 %reduce-scatter.3.cloned.1.call-start = ((), (), s32[]{:S(2)}) async-start(), calls=%async_computation.6 | async-start | bytes 6291456 | tf_op jit(solution)/shard_map/reduce_scatter | solution.py:106
  86.7 3.1 %copy-start.4 = (bf16[2,2048,512]{2,1,0:T(8,128)(2,1)S(1)}, bf16[2,2048,512]{2,1,0:T(8,128)(2,1)}, u32[]{:S(2)}) copy-start(bf16[2,2048,512]{2,1,0:T(8,128)(2,1)} %all-gather.2.cloned.1.call-done) | copy-start | bytes 12582916
  89.7 2.9 %copy-start.8 = (bf16[512,2048]{1,0:T(8,128)(2,1)}, bf16[512,2048]{1,0:T(8,128)(2,1)S(1)}, u32[]{:S(2)}) copy-start(bf16[512,2048]{1,0:T(8,128)(2,1)S(1)} %get-tuple-element.16) | copy-start | bytes 6291460
  92.6 1.3 copy-start.10
  97.6 14.6 %copy-start.11 = (bf16[512,2048]{1,0:T(8,128)(2,1)S(1)}, bf16[512,2048]{1,0:T(8,128)(2,1)}, u32[]{:S(2)}) copy-start(bf16[512,2048]{1,0:T(8,128)(2,1)} %copy-done.10) | copy-start | bytes 6291460
  97.6 64.7 %reduce-scatter.5.cloned.1.call-start = ((), (), s32[]{:S(2)}) async-start(), calls=%async_computation.7 | async-start | bytes 2621440 | tf_op jit(solution)/shard_map/reduce_scatter | solution.py:105
  112.2 3.0 %copy-start.5 = (bf16[2,2048,512]{2,1,0:T(8,128)(2,1)S(1)}, bf16[2,2048,512]{2,1,0:T(8,128)(2,1)}, u32[]{:S(2)}) copy-start(bf16[2,2048,512]{2,1,0:T(8,128)(2,1)} %all-gather.2.cloned.1.call-done) | copy-start | bytes 12582916
  112.2 3.5 %copy-start.9 = (bf16[512,2048]{1,0:T(8,128)(2,1)S(1)}, bf16[512,2048]{1,0:T(8,128)(2,1)}, u32[]{:S(2)}) copy-start(bf16[512,2048]{1,0:T(8,128)(2,1)} %copy-done.8) | copy-start | bytes 6291460
Sparse Core Ops, SparseCore 0:
  40.5 26.1 all-gather.1
  97.7 14.3 reduce-scatter.2
  115.2 34.4 reduce-scatter.4
